TPU v7x, 256 devices: a whole 4x4x8 slice. The times are simulated.
256 devices in a mesh: rows: 64 (over y, z, core), rhs: 4 (over x).
Axes of the slice: x: 4, y: 4, z: 8, core: 2. Of those that a mesh axis runs over, the one named last changes fastest.
Arguments:
- kernel_rows: bfloat16 [131072, 512], P(('rows', 'rhs')), may hold values from 0 to 1
- factor_blocks: bfloat16 [512, 8, 256, 256], P('rows'), may hold values from -0.125 to 0.125
- diag_inverse: bfloat16 [512, 256, 256], P('rows'), as said below
- pattern: int32 [512, 8], P('rows'), may hold values from 0 to 511, as said below
- live_counts: int32 [512], P('rows'), may hold values from 0 to 8, as said below
Outputs:
- solution: bfloat16 [131072, 512], P('rows', 'rhs')
Inputs may be any that keep to these rules, and one draw needn't show every extreme that they name: pattern[s, k] names a block row of a lower level than s; slot 0 of every block row above level 0 names a block row of the level just below; rows of level 0 hold 0. Block row t is held by index t // 8 of rows; the used slots of the block rows held by one index of rows name, for any one level, at most 1 distinct block rows held by any one other index. `live_counts`: 0 on level 0, from 1 to 8 on higher levels, 8 reached. `diag_inverse`: each block is the inverse of a well-conditioned diagonal block of the factor.
All inputs are finite; a program needn't handle non-finite values.
Results may differ from a plain program's by a relative error of at most 0.0058.
Values may be sent and summed in bfloat16 or wider, within the bound.
No kernel may reach another device: no remote copies, remote signals or barrier semaphores. Data moves between devices by JAX's collectives and lax.ppermute only.
A program may use at most 128 MiB of HBM per device.

v0:
```python
import jax
import jax.numpy as jnp
from jax import lax
from jax.sharding import PartitionSpec as P

LEV = 4


def shards(kernel_rows, factor_blocks, diag_inverse, pattern, live_counts):
    received = lax.all_to_all(kernel_rows, "rhs", split_axis=1, concat_axis=0, tiled=True)
    per_device = factor_blocks.shape[0]
    slot_count = factor_blocks.shape[1]
    block = factor_blocks.shape[2]
    width = received.shape[1]
    right_side = received.reshape(per_device, block, width)
    holders = lax.axis_size("rows")
    per_level = per_device // LEV
    level_size = holders * per_level
    level_of = pattern % per_device // per_level
    holder_of = pattern // per_device
    offset_of = pattern % per_level
    active = jnp.arange(slot_count)[None, :] < live_counts[:, None]
    position = holder_of * per_level + offset_of
    flat_index = level_of * level_size + position
    gathered_all = []
    solved_all = []
    for level_now in range(LEV):
        lower = level_now * per_level
        upper = lower + per_level
        if level_now == 0:
            summed_now = jnp.zeros((per_level, block, width), jnp.float32)
        else:
            available = jnp.concatenate(gathered_all, axis=0)
            picked = jnp.take(available, flat_index[lower:upper], axis=0, mode="clip")
            picked = jnp.where(active[lower:upper, :, None, None], picked, jnp.zeros_like(picked))
            summed_now = jnp.einsum(
                "bkij,bkjr->bir",
                factor_blocks[lower:upper],
                picked,
                preferred_element_type=jnp.float32,
            )
        residual = (right_side[lower:upper].astype(jnp.float32) - summed_now).astype(jnp.bfloat16)
        solved = jnp.einsum(
            "bij,bjr->bir", diag_inverse[lower:upper], residual, preferred_element_type=jnp.float32
        ).astype(jnp.bfloat16)
        solved_all.append(solved)
        if level_now + 1 < LEV:
            incoming = lax.all_gather(solved, "rows", axis=0, tiled=True)
            gathered_all.append(incoming)
    return jnp.concatenate(solved_all, axis=0).reshape(per_device * block, width)


def solution(mesh):
    placed = (
        P(("rows", "rhs"), None),
        P("rows", None, None, None),
        P("rows", None, None),
        P("rows", None),
        P("rows"),
    )
    return jax.shard_map(
        shards, mesh=mesh, in_specs=placed, out_specs=P("rows", "rhs"), check_vma=False
    )
```

profile of v0, /device:TPU:1, one launch (start us, length us, event | category | flops | bytes accessed | tf_op | source)
XLA Modules:
  0.0 339.4 jit_solution(18205425547887080133)
XLA Ops:
  6.5 0.0 all-gather.4.cloned.1.call-start
  6.5 1.3 copy.30
  7.8 13.2 %all_to_all.16 = bf16[512,4,128]{0,2,1:T(8,128)(2,1)S(1)} all-to-all(bf16[512,4,128]{0,2,1:T(8,128)(2,1)S(1)} %bitcast.60), channel_id=1, replica_groups=mesh['rows'=64,'rhs'=4] {'rhs'}, dimensions={1} | all-to-all | bytes 1048576 | tf_op jit(solution)/shard_map/all_to_all | solution.py:10
  21.0 0.1 fusion.84
  21.0 0.1 copy.31
  21.2 1.8 convolution_convert_fusion
  23.0 0.0 all-gather.4.cloned.1.call-update
  23.0 0.0 all-gather.6.cloned.1.call-start
  23.1 0.7 fusion.71
  23.8 0.1 reshape.28
  23.9 0.7 iota_compare_fusion
  24.6 0.1 copy.32
  24.7 0.1 copy.34
  24.9 84.1 %all-gather.4.cloned.1.call-done = bf16[128,256,128]{2,1,0:T(8,128)(2,1)} async-done(((bf16[2,256,128]{2,1,0:T(8,128)(2,1)}), bf16[128,256,128]{2,1,0:T(8,128)(2,1)}) %all-gather.4.cloned.1.call-update) | async-done | bytes 8388624 | tf_op jit(solution)/shard_map/all_gather | solution.py:48
  109.0 4.1 %gather_fusion = bf16[16,256,128]{2,1,0:T(8,128)(2,1)S(1)} fusion(bf16[128,256,128]{2,1,0:T(8,128)(2,1)} %all-gather.4.cloned.1.call-done, s32[1024]{0:T(1024)S(1)} %pad_clamp_fusion.2), kind=kCustom, calls=%fused_computation | custom fusion | bytes 2097216 | tf_op jit(solution)/shard_map/jit(_take)/gather | solution.py:34
  113.1 0.5 copy.33
  113.7 3.3 fusion.39
  116.9 0.0 all-gather.6.cloned.1.call-update
  117.0 0.0 all-gather.8.cloned.1.call-start
  117.0 0.1 reshape.36
  117.1 0.1 copy.36
  117.2 0.8 copy.38
  118.1 0.0 copy-start.3
  118.1 79.3 %all-gather.6.cloned.1.call-done = bf16[128,256,128]{2,1,0:T(8,128)(2,1)} async-done(((bf16[2,256,128]{2,1,0:T(8,128)(2,1)}), bf16[128,256,128]{2,1,0:T(8,128)(2,1)}) %all-gather.6.cloned.1.call-update) | async-done | bytes 8388624 | tf_op jit(solution)/shard_map/all_gather | solution.py:48
  197.4 13.9 %pad_maximum_fusion.1 = bf16[256,256,128]{2,1,0:T(8,128)(2,1)} fusion(bf16[128,256,128]{2,1,0:T(8,128)(2,1)} %all-gather.6.cloned.1.call-done, bf16[128,256,128]{2,1,0:T(8,128)(2,1)} %all-gather.4.cloned.1.call-done), kind=kLoop, calls=%fused_computation.4 | loop fusion | flops 8388608 | bytes 33554432 | tf_op jit(solution)/shard_map/concatenate | solution.py:33
  211.3 6.5 %gather_fusion.1 = bf16[16,256,128]{2,1,0:T(8,128)(2,1)S(1)} fusion(bf16[256,256,128]{2,1,0:T(8,128)(2,1)} %pad_maximum_fusion.1, s32[1024]{0:T(1024)S(1)} %pad_clamp_fusion.1), kind=kCustom, calls=%fused_computation.1 | custom fusion | bytes 2097216 | tf_op jit(solution)/shard_map/jit(_take)/gather | solution.py:34
  217.8 0.5 copy.37
  218.4 0.0 copy-done.3
  218.4 3.3 fusion.42
  221.7 0.0 all-gather.8.cloned.1.call-update
  221.7 0.1 reshape.44
  221.8 0.1 copy.40
  221.9 0.8 copy.42
  222.7 79.4 %all-gather.8.cloned.1.call-done = bf16[128,256,128]{2,1,0:T(8,128)(2,1)} async-done(((bf16[2,256,128]{2,1,0:T(8,128)(2,1)}), bf16[128,256,128]{2,1,0:T(8,128)(2,1)}) %all-gather.8.cloned.1.call-update) | async-done | bytes 8388624 | tf_op jit(solution)/shard_map/all_gather | solution.py:48
  302.1 17.7 %pad_maximum_fusion = bf16[384,256,128]{2,1,0:T(8,128)(2,1)} fusion(bf16[128,256,128]{2,1,0:T(8,128)(2,1)} %all-gather.8.cloned.1.call-done, bf16[128,256,128]{2,1,0:T(8,128)(2,1)} %all-gather.6.cloned.1.call-done, bf16[128,256,128]{2,1,0:T(8,128)(2,1)} %all-gather.4.cloned.1.call-done), kind=kLoop, calls=%fused_computation.3 | loop fusion | flops 25165824 | bytes 50331648 | tf_op jit(solution)/shard_map/concatenate | solution.py:33
  319.8 0.0 copy-start
  319.9 0.0 copy-start.1
  319.9 0.0 copy-start.2
  319.9 9.0 %gather_fusion.2 = bf16[16,256,128]{2,1,0:T(8,128)(2,1)S(1)} fusion(bf16[384,256,128]{2,1,0:T(8,128)(2,1)} %pad_maximum_fusion, s32[1024]{0:T(1024)S(1)} %pad_clamp_fusion), kind=kCustom, calls=%fused_computation.2 | custom fusion | bytes 2097216 | tf_op jit(solution)/shard_map/jit(_take)/gather | solution.py:34
  328.8 0.5 copy.41
  329.4 2.6 fusion.45
  332.0 0.0 copy-done
  332.0 0.0 copy-done.1
  332.0 0.0 copy-done.2
  332.0 0.9 pad_maximum_fusion.2
  (5 shorter events, 0.0 us)
Async XLA Ops:
  6.5 102.5 %all-gather.4.cloned.1.call-start = ((), (), s32[]{:S(2)}) async-start(), calls=%async_computation.1 | async-start | bytes 8519680 | tf_op jit(solution)/shard_map/all_gather | solution.py:48
  23.0 174.4 %all-gather.6.cloned.1.call-start = ((), (), s32[]{:S(2)}) async-start(), calls=%async_computation.2 | async-start | bytes 8519680 | tf_op jit(solution)/shard_map/all_gather | solution.py:48
  117.0 185.2 %all-gather.8.cloned.1.call-start = ((), (), s32[]{:S(2)}) async-start(), calls=%async_computation.3 | async-start | bytes 8519680 | tf_op jit(solution)/shard_map/all_gather | solution.py:48
  118.1 100.3 %copy-start.3 = (bf16[8,256,256]{2,1,0:T(8,128)(2,1)S(1)}, bf16[8,256,256]{2,1,0:T(8,128)(2,1)}, u32[]{:S(2)}) copy-start(bf16[8,256,256]{2,1,0:T(8,128)(2,1)} %param.7) | copy-start | bytes 3145732
  319.8 12.2 %copy-start = (bf16[2,256,128]{2,1,0:T(8,128)(2,1)S(1)}, bf16[2,256,128]{2,1,0:T(8,128)(2,1)}, u32[]{:S(2)}) copy-start(bf16[2,256,128]{2,1,0:T(8,128)(2,1)} %convolution_convert_fusion) | copy-start | bytes 393220
  319.9 12.2 %copy-start.1 = (bf16[2,256,128]{2,1,0:T(8,128)(2,1)S(1)}, bf16[2,256,128]{2,1,0:T(8,128)(2,1)}, u32[]{:S(2)}) copy-start(bf16[2,256,128]{2,1,0:T(8,128)(2,1)} %fusion.39) | copy-start | bytes 393220
  319.9 12.2 %copy-start.2 = (bf16[2,256,128]{2,1,0:T(8,128)(2,1)S(1)}, bf16[2,256,128]{2,1,0:T(8,128)(2,1)}, u32[]{:S(2)}) copy-start(bf16[2,256,128]{2,1,0:T(8,128)(2,1)} %fusion.42) | copy-start | bytes 393220
Sparse Core Ops, SparseCore 0:
  23.1 85.8 all-gather.3
  117.1 80.2 all-gather.5
  221.8 80.2 all-gather.7
where the time goes:
time: 340 us; the launch traced here: 339 us
  waiting for transfers between devices  243 us (71%)
  other arithmetic  34 us (10%)
  local copies, waits for them, and re-layouts  25 us (7%)
  between operations  13.3 us (4%)
  blocking collectives  13.2 us (4%)
  matrix products  11 us (3%)
    all_gather x3, waiting for transfers between devices, shards(): incoming = lax.all_gather(solved, 'rows', axis=0, tiled=True)  243 us
    concatenate x2, other arithmetic, shards(): available = jnp.concatenate(gathered_all, axis=0)  31.6 us
    gather x6, local copies, waits for them, and re-layouts, shards(): picked = jnp.take(available, flat_index[lower:upper], axis=0, mode='clip')  21.2 us
    all_to_all x1, blocking collectives, shards(): lax.all_to_all(kernel_rows, 'rhs', split_axis=1, concat_axis=0, tiled=True)  13.2 us
    dot_general x4, matrix products, shards(): jnp.einsum('bij,bjr->bir', diag_inverse[lower:upper], residual, preferred...  11 us
  transfers between devices with their start and end apart: 3, of which 3 were waited for; matrix products, arithmetic and copies ran while one was open for 1% of the time, Pallas kernels for 0%

commit v1 on v0

--- a/solution.py
+++ b/solution.py
@@ -45,7 +45,9 @@
         ).astype(jnp.bfloat16)
         solved_all.append(solved)
         if level_now + 1 < LEV:
-            incoming = lax.all_gather(solved, "rows", axis=0, tiled=True)
+            incoming = jnp.concatenate(
+                lax.all_to_all(jnp.stack([solved] * lax.axis_size("rows")), "rows", 0, 0), axis=0
+            )
             gathered_all.append(incoming)
     return jnp.concatenate(solved_all, axis=0).reshape(per_device * block, width)
 

time: 340 us -> 677 us (1.99)
  waiting for transfers between devices: 243 us -> 556 us
  starting transfers between devices: 0.09 us -> 26.1 us
  local copies, waits for them, and re-layouts: 25 us -> 39.5 us
  between operations: 13.3 us -> 0.2 us
    all_to_all x0 -> x3, waiting for transfers between devices: none -> 556 us  [shards(): lax.all_to_all(jnp.stack([solved] * lax.axis_size('rows')), 'rows', 0, 0)]
    all_gather x3 -> x0, waiting for transfers between devices: 243 us -> none  [shards(): incoming = lax.all_gather(solved, 'rows', axis=0, tiled=True)]
    all_to_all x0 -> x3, starting transfers between devices: none -> 26.1 us  [shards(): lax.all_to_all(jnp.stack([solved] * lax.axis_size('rows')), 'rows', 0, 0)]
    another operation x0 -> x3, local copies, waits for them, and re-layouts: none -> 15.9 us  [shards(): jnp.stack([solved] * lax.axis_size('rows'))]
  transfers between devices with their start and end apart: 3 -> 3, of which waited for: 3 -> 3; matrix products, arithmetic and copies ran while one was open for 1% -> 0% of each run, Pallas kernels for 0% -> 0%
where the time goes in v1:
time: 677 us
  waiting for transfers between devices  556 us (82%)
  local copies, waits for them, and re-layouts  39.5 us (6%)
  other arithmetic  32.7 us (5%)
  starting transfers between devices  26.1 us (4%)
  blocking collectives  13.2 us (2%)
  matrix products  9.03 us (1%)
    all_to_all x3, waiting for transfers between devices, shards(): lax.all_to_all(jnp.stack([solved] * lax.axis_size('rows')), 'rows', 0, 0)  556 us
    concatenate x2, other arithmetic, shards(): available = jnp.concatenate(gathered_all, axis=0)  31.6 us
    all_to_all x3, starting transfers between devices, shards(): lax.all_to_all(jnp.stack([solved] * lax.axis_size('rows')), 'rows', 0, 0)  26.1 us
    gather x6, local copies, waits for them, and re-layouts, shards(): picked = jnp.take(available, flat_index[lower:upper], axis=0, mode='clip')  21.1 us
    another operation x3, local copies, waits for them, and re-layouts, shards(): jnp.stack([solved] * lax.axis_size('rows'))  15.9 us
  transfers between devices with their start and end apart: 3, of which 3 were waited for; matrix products, arithmetic and copies ran while one was open for 0% of the time, Pallas kernels for 0%

profile of v1, /device:TPU:1, one launch (start us, length us, event | category | flops | bytes accessed | tf_op | source)
XLA Modules:
  0.0 676.7 jit_solution(8379123917047182387)
XLA Ops:
  0.0 1.3 copy.27
  1.3 13.2 %all_to_all.31 = bf16[512,4,128]{0,2,1:T(8,128)(2,1)S(1)} all-to-all(bf16[512,4,128]{0,2,1:T(8,128)(2,1)S(1)} %bitcast.63), channel_id=1, replica_groups=mesh['rows'=64,'rhs'=4] {'rhs'}, dimensions={1} | all-to-all | bytes 1048576 | tf_op jit(solution)/shard_map/all_to_all | solution.py:10
  14.4 0.1 fusion.84
  14.5 0.1 copy.28
  14.6 1.2 convolution_convert_fusion
  15.8 5.3 stack.6
  21.1 0.0 copy-start
  21.1 0.0 copy-start.1
  21.1 13.9 %all-to-all-start.1 = ((bf16[64,2,256,128]{3,2,1,0:T(8,128)(2,1)}), bf16[64,2,256,128]{3,2,1,0:T(8,128)(2,1)}, u32[]{:S(2)}, u32[]{:S(2)}) async-start(bf16[64,2,256,128]{3,2,1,0:T(8,128)(2,1)} %stack.6), calls=%async_computation.1 | async-start | bytes 16777216 | tf_op jit(solution)/shard_map/all_to_all | solution.py:49
  35.0 0.0 copy-done
  35.1 0.1 reshape.46
  35.2 0.0 copy-done.1
  35.2 0.1 iota_compare_fusion
  35.2 0.1 copy.29
  35.4 0.1 copy.31
  35.5 185.3 %all-to-all-done.1 = bf16[64,2,256,128]{3,2,1,0:T(8,128)(2,1)} async-done(((bf16[64,2,256,128]{3,2,1,0:T(8,128)(2,1)}), bf16[64,2,256,128]{3,2,1,0:T(8,128)(2,1)}, u32[]{:S(2)}, u32[]{:S(2)}) %all-to-all-start.1) | async-done | bytes 8388640 | tf_op jit(solution)/shard_map/all_to_all | solution.py:49
  220.8 4.1 gather_fusion
  224.9 0.5 copy.30
  225.5 2.6 fusion.39
  228.1 5.3 stack.7
  233.4 6.1 all-to-all-start.2
  239.5 0.1 reshape.54
  239.6 0.1 copy.33
  239.7 0.1 copy.35
  239.9 185.4 %all-to-all-done.2 = bf16[64,2,256,128]{3,2,1,0:T(8,128)(2,1)} async-done(((bf16[64,2,256,128]{3,2,1,0:T(8,128)(2,1)}), bf16[64,2,256,128]{3,2,1,0:T(8,128)(2,1)}, u32[]{:S(2)}, u32[]{:S(2)}) %all-to-all-start.2) | async-done | bytes 8388640 | tf_op jit(solution)/shard_map/all_to_all | solution.py:49
  425.3 13.9 %pad_maximum_fusion.1 = bf16[256,256,128]{2,1,0:T(8,128)(2,1)} fusion(bf16[128,256,128]{2,1,0:T(8,128)(2,1)} %bitcast.11, bf16[128,256,128]{2,1,0:T(8,128)(2,1)} %bitcast.4), kind=kLoop, calls=%fused_computation.4 | loop fusion | flops 8388608 | bytes 33554432 | tf_op jit(solution)/shard_map/concatenate | solution.py:33
  439.2 6.5 gather_fusion.1
  445.7 0.5 copy.34
  446.3 2.6 fusion.42
  448.9 5.3 stack.8
  454.2 6.1 all-to-all-start.3
  460.3 0.1 reshape.62
  460.4 0.1 copy.37
  460.5 0.1 copy.39
  460.6 185.4 %all-to-all-done.3 = bf16[64,2,256,128]{3,2,1,0:T(8,128)(2,1)} async-done(((bf16[64,2,256,128]{3,2,1,0:T(8,128)(2,1)}), bf16[64,2,256,128]{3,2,1,0:T(8,128)(2,1)}, u32[]{:S(2)}, u32[]{:S(2)}) %all-to-all-start.3) | async-done | bytes 8388640 | tf_op jit(solution)/shard_map/all_to_all | solution.py:49
  646.1 17.7 %pad_maximum_fusion = bf16[384,256,128]{2,1,0:T(8,128)(2,1)} fusion(bf16[128,256,128]{2,1,0:T(8,128)(2,1)} %bitcast.18, bf16[128,256,128]{2,1,0:T(8,128)(2,1)} %bitcast.11, bf16[128,256,128]{2,1,0:T(8,128)(2,1)} %bitcast.4), kind=kLoop, calls=%fused_computation.3 | loop fusion | flops 25165824 | bytes 50331648 | tf_op jit(solution)/shard_map/concatenate | solution.py:33
  663.8 8.9 %gather_fusion.2 = bf16[16,256,128]{2,1,0:T(8,128)(2,1)S(1)} fusion(bf16[384,256,128]{2,1,0:T(8,128)(2,1)} %pad_maximum_fusion, s32[1024]{0:T(1024)S(1)} %pad_clamp_fusion), kind=kCustom, calls=%fused_computation.2 | custom fusion | bytes 2097216 | tf_op jit(solution)/shard_map/jit(_take)/gather | solution.py:34
  672.7 0.5 copy.38
  673.2 2.6 fusion.45
  675.8 0.9 pad_maximum_fusion.2
  (6 shorter events, 0.1 us)
Async XLA Ops:
  21.1 13.9 %copy-start = (s32[8,8]{1,0:T(8,128)S(1)}, s32[8,8]{1,0:T(8,128)}, u32[]{:S(2)}) copy-start(s32[8,8]{1,0:T(8,128)} %param.8) | copy-start | bytes 772
  21.1 14.0 %copy-start.1 = (s32[8]{0:T(128)S(1)}, s32[8]{0:T(128)}, u32[]{:S(2)}) copy-start(s32[8]{0:T(128)} %param.9) | copy-start | bytes 100
  21.1 199.7 %all-to-all-start.1 = ((bf16[64,2,256,128]{3,2,1,0:T(8,128)(2,1)}), bf16[64,2,256,128]{3,2,1,0:T(8,128)(2,1)}, u32[]{:S(2)}, u32[]{:S(2)}) async-start(bf16[64,2,256,128]{3,2,1,0:T(8,128)(2,1)} %stack.6), calls=%async_computation.1 | async-start | bytes 16777216 | tf_op jit(solution)/shard_map/all_to_all | solution.py:49
  233.4 191.9 %all-to-all-start.2 = ((bf16[64,2,256,128]{3,2,1,0:T(8,128)(2,1)}), bf16[64,2,256,128]{3,2,1,0:T(8,128)(2,1)}, u32[]{:S(2)}, u32[]{:S(2)}) async-start(bf16[64,2,256,128]{3,2,1,0:T(8,128)(2,1)} %stack.7), calls=%async_computation.2 | async-start | bytes 16777216 | tf_op jit(solution)/shard_map/all_to_all | solution.py:49
  454.2 191.9 %all-to-all-start.3 = ((bf16[64,2,256,128]{3,2,1,0:T(8,128)(2,1)}), bf16[64,2,256,128]{3,2,1,0:T(8,128)(2,1)}, u32[]{:S(2)}, u32[]{:S(2)}) async-start(bf16[64,2,256,128]{3,2,1,0:T(8,128)(2,1)} %stack.8), calls=%async_computation.3 | async-start | bytes 16777216 | tf_op jit(solution)/shard_map/all_to_all | solution.py:49
